TPU v7x, 256 devices: a whole 4x4x8 slice. The times are simulated.
256 devices in a mesh: row: 8 (over z), col: 32 (over y, x, core).
Axes of the slice: x: 4, y: 4, z: 8, core: 2. Of those that a mesh axis runs over, the one named last changes fastest.
Arguments:
- hidden_in: bfloat16 [1024, 2304], P('row', 'col'), may hold values from -40 to 40
- attn_gain: float32 [2304], P('col'), may hold values from 0.1 to 1.9
- qkv_weight: bfloat16 [2304, 6912], P('col'), may hold values from -0.125 to 0.125
- out_weight: bfloat16 [2304, 2304], P(None, 'col'), may hold values from -0.125 to 0.125
- moe_gain: float32 [2304], P('col'), may hold values from 0.1 to 1.9
- router_weight: float32 [2304, 8], P('col'), may hold values from -0.125 to 0.125
- expert_gate: bfloat16 [8, 2304, 5760], P('row', None, 'col'), may hold values from -0.125 to 0.125
- expert_up: bfloat16 [8, 2304, 5760], P('row', None, 'col'), may hold values from -0.125 to 0.125
- expert_down: bfloat16 [8, 5760, 2304], P('row', 'col'), may hold values from -0.078125 to 0.078125
- cache_keys: bfloat16 [2048, 64, 2304], P(('row', 'col')), may hold values from -400 to 400
- cache_values: bfloat16 [2048, 64, 2304], P(('row', 'col')), may hold values from -12 to 12
- block_table: int32 [8, 4, 64], P('row'), may hold values from 0 to 2047, as said below
- prefix_lengths: int32 [8, 4], P('row'), may hold values from 1024 to 4096, as said below
- prompt_lengths: int32 [8, 4], P('row'), may hold values from 1 to 64, 128 in all within a row
- routed_experts: int32 [1024, 2], P('row'), may hold values from 0 to 7, all different within a row; in each aligned block of 128 rows (0 to 127, 128 to 255, ...) at most 64 rows name the same one
Outputs:
- attn_out: bfloat16 [1024, 2304], P('row', 'col')
- moe_out: bfloat16 [1024, 2304], P('row', 'col')
- layer_out: bfloat16 [1024, 2304], P('row', 'col')
Inputs may be any that keep to these rules, and one draw needn't show every extreme that they name: `block_table`: entry [g, q, j] lies among the 8 pages that begin at (g * 32 + j % 32) * 8; the entries that fall among the same 8 pages are distinct. `prefix_lengths`: some request has exactly 4096 cached tokens. `prompt_lengths`: the 4 lengths of a group sum to 128; the longest of each group is exactly 64. `routed_experts`: the 2 experts of a token differ; among the tokens of one group no expert is named more than 64 times, and in some group an expert reaches 64; every expert is named by some token.
All inputs are finite; a program needn't handle non-finite values.
Results may differ from a plain program's by a relative error of at most 0.02.
The roundings to bfloat16 on the way count: a program that leaves them out, or rounds other values in their place, can miss the bound.
Values may be sent and summed in bfloat16 or wider, within the bound.
No kernel may reach another device: no remote copies, remote signals or barrier semaphores. Data moves between devices by JAX's collectives and lax.ppermute only.
A program may use at most 192 MiB of HBM per device.

v0:
```python
import math
import jax
import jax.numpy as jnp
from jax import lax
from jax.sharding import PartitionSpec as P

D = 2304
HEAD_DIM = 64
TOP = 2
norm_epsilon = 1e-05
residual_scale = 1.4 / math.sqrt(40.0)
rotary_base = 10000.0
masked_score = -1e30


def merged(value, axis, join):
    pieces = jax.tree.map(lambda part: lax.all_gather(part, axis), value)
    head = jax.tree.map(lambda part: part[0], pieces)
    tail = jax.tree.map(lambda part: part[1:], pieces)
    running, _ = lax.scan(lambda running, slab: (join(running, slab), None), head, tail)
    return running


def rotate(values, positions, head_dim):
    row_count = values.shape[0]
    head_count = values.shape[1] // head_dim
    half_dim = head_dim // 2
    frequency = rotary_base ** (-2.0 * jnp.arange(half_dim, dtype=jnp.float32) / head_dim)
    angles = positions.astype(jnp.float32)[:, None] * frequency[None, :]
    cosine = jnp.cos(angles)[:, None, :]
    sine_part = jnp.sin(angles)[:, None, :]
    shaped = values.reshape(row_count, head_count, head_dim)
    first_half = shaped[:, :, :half_dim]
    second_half = shaped[:, :, half_dim:]
    turned = jnp.concatenate(
        [
            first_half * cosine - second_half * sine_part,
            second_half * cosine + first_half * sine_part,
        ],
        axis=2,
    )
    return turned.reshape(row_count, head_count * head_dim)


def token_layout(prompt_row, prefix_row, row_count):
    run_ends = jnp.cumsum(prompt_row, dtype=jnp.int32)
    starts = run_ends - prompt_row
    offsets = jnp.arange(row_count, dtype=jnp.int32)
    request = jnp.sum(
        (offsets[:, None] >= run_ends[None, :]).astype(jnp.int32), axis=1, dtype=jnp.int32
    )
    member = request[:, None] == jnp.arange(prompt_row.shape[0], dtype=jnp.int32)[None, :]
    start_of = jnp.sum(jnp.where(member, starts[None, :], 0), axis=1, dtype=jnp.int32)
    prefix_of = jnp.sum(jnp.where(member, prefix_row[None, :], 0), axis=1, dtype=jnp.int32)
    return (request, prefix_of + offsets - start_of)


def rescale(summed, factor):
    group_count, row_count, feature_width = summed.shape
    group_size = factor.shape[1]
    shaped = summed.reshape(group_count, row_count, group_size, feature_width // group_size)
    shaped = shaped * jnp.transpose(factor, (0, 2, 1))[:, :, :, None]
    return shaped.reshape(group_count, row_count, feature_width)


def divide_rows(summed, total_weight):
    group_count, row_count, feature_width = summed.shape
    group_size = total_weight.shape[1]
    shaped = summed.reshape(group_count, row_count, group_size, feature_width // group_size)
    shaped = shaped / jnp.transpose(total_weight, (0, 2, 1))[:, :, :, None]
    return shaped.reshape(group_count, row_count, feature_width)


def combine_parts(earlier_part, later_part):
    largest = jnp.maximum(earlier_part[0], later_part[0])
    factor_one = jnp.exp(earlier_part[0] - largest)
    factor_two = jnp.exp(later_part[0] - largest)
    total_weight = earlier_part[1] * factor_one + later_part[1] * factor_two
    summed = rescale(earlier_part[2], factor_one) + rescale(later_part[2], factor_two)
    return (largest, total_weight, summed)


def on_device(
    hidden_in,
    attn_gain,
    qkv_weight,
    out_weight,
    moe_gain,
    router_weight,
    expert_gate,
    expert_up,
    expert_down,
    cache_keys,
    cache_values,
    block_table,
    prefix_lengths,
    prompt_lengths,
    routed_experts,
):
    col_count = lax.axis_size("col")
    row_devices = lax.axis_size("row")
    col_index = lax.axis_index("col")
    row_index = lax.axis_index("row")
    tok_rows = hidden_in.shape[0]
    feature_width = hidden_in.shape[1]
    head_total = out_weight.shape[0]
    head_count = head_total // HEAD_DIM
    key_share = tok_rows // col_count
    request, position = token_layout(prompt_lengths[0], prefix_lengths[0], tok_rows)
    own_start = col_index * key_share
    key_position = lax.dynamic_slice_in_dim(position, own_start, key_share)
    key_request = lax.dynamic_slice_in_dim(request, own_start, key_share)
    residual = hidden_in.astype(jnp.float32)
    squares = lax.psum(jnp.sum(residual * residual, axis=1), "col")
    scale_one = lax.rsqrt(squares / D + norm_epsilon)
    normed = (residual * scale_one[:, None] * attn_gain[None, :]).astype(jnp.bfloat16)
    query_part = jnp.dot(normed, qkv_weight[:, :head_total], preferred_element_type=jnp.float32)
    query_sum = lax.psum(query_part, "col")
    queries = (rotate(query_sum, position, HEAD_DIM) * HEAD_DIM ** (-0.5)).astype(jnp.bfloat16)
    key_value = lax.psum_scatter(
        jnp.dot(normed, qkv_weight[:, head_total:], preferred_element_type=jnp.float32).astype(
            jnp.bfloat16
        ),
        "col",
        scatter_dimension=0,
        tiled=True,
    ).astype(jnp.float32)
    new_keys = rotate(key_value[:, :head_total], key_position, HEAD_DIM).astype(jnp.bfloat16)
    new_values = key_value[:, head_total:].astype(jnp.bfloat16)
    pool_size = cache_keys.shape[0]
    page_size = cache_keys.shape[1]
    req_count = block_table.shape[1]
    pages_each = block_table.shape[2] // col_count
    page_table = block_table[0].reshape(req_count, pages_each, col_count)
    own_pages = lax.dynamic_slice_in_dim(page_table, col_index, 1, 2).reshape(
        req_count * pages_each
    )
    pool_offset_begin = (row_index * col_count + col_index) * pool_size
    slot_ids = jnp.arange(pool_size, dtype=jnp.int32)
    entry_ids = jnp.arange(req_count * pages_each, dtype=jnp.int32)
    slot_match = (own_pages - pool_offset_begin)[None, :] == slot_ids[:, None]
    entry_request = entry_ids // pages_each
    entry_page = entry_ids % pages_each * col_count + col_index
    slot_request = jnp.sum(
        jnp.where(slot_match, entry_request[None, :], 0), axis=1, dtype=jnp.int32
    )
    slot_page = jnp.sum(jnp.where(slot_match, entry_page[None, :], 0), axis=1, dtype=jnp.int32)
    prefix_row = prefix_lengths[0]
    slot_prefix = jnp.sum(
        jnp.where(
            slot_request[:, None] == jnp.arange(req_count, dtype=jnp.int32)[None, :],
            prefix_row[None, :],
            0,
        ),
        axis=1,
        dtype=jnp.int32,
    )
    cache_position = (
        slot_page[:, None] * page_size + jnp.arange(page_size, dtype=jnp.int32)[None, :]
    )
    cache_live = (
        (cache_position < slot_prefix[:, None]).astype(jnp.int32).reshape(pool_size * page_size)
    )
    cache_request = jnp.broadcast_to(slot_request[:, None], (pool_size, page_size)).reshape(
        pool_size * page_size
    )
    cache_mask = (request[:, None] == cache_request[None, :]) & (cache_live[None, :] > 0)
    fresh_mask = (request[:, None] == key_request[None, :]) & (
        key_position[None, :] <= position[:, None]
    )
    group_size = math.gcd(head_count, 4)
    group_count = head_count // group_size
    query_heads = queries.reshape(tok_rows, head_count, HEAD_DIM)
    cached_key_heads = cache_keys.reshape(pool_size * page_size, head_count, HEAD_DIM)
    cached_value_heads = cache_values.reshape(pool_size * page_size, head_count, HEAD_DIM)
    fresh_key_heads = new_keys.reshape(key_share, head_count, HEAD_DIM)
    fresh_value_heads = new_values.reshape(key_share, head_count, HEAD_DIM)

    def head_group(group_index):
        first_head = group_index * group_size
        query_piece = lax.dynamic_slice_in_dim(query_heads, first_head, group_size, 1)
        key_piece = lax.dynamic_slice_in_dim(cached_key_heads, first_head, group_size, 1)
        value_piece = lax.dynamic_slice_in_dim(cached_value_heads, first_head, group_size, 1)
        fresh_key_piece = lax.dynamic_slice_in_dim(fresh_key_heads, first_head, group_size, 1)
        fresh_value_piece = lax.dynamic_slice_in_dim(fresh_value_heads, first_head, group_size, 1)
        score_matrix = jnp.einsum(
            "thd,khd->htk", query_piece, key_piece, preferred_element_type=jnp.float32
        )
        score_matrix = jnp.where(cache_mask[None], score_matrix, masked_score)
        fresh_scores = jnp.einsum(
            "thd,khd->htk", query_piece, fresh_key_piece, preferred_element_type=jnp.float32
        )
        fresh_scores = jnp.where(fresh_mask[None], fresh_scores, masked_score)
        largest = jnp.maximum(jnp.max(score_matrix, axis=2), jnp.max(fresh_scores, axis=2))
        cached_exp = jnp.where(cache_mask[None], jnp.exp(score_matrix - largest[:, :, None]), 0.0)
        fresh_exp = jnp.where(fresh_mask[None], jnp.exp(fresh_scores - largest[:, :, None]), 0.0)
        total_weight = jnp.sum(cached_exp, axis=2) + jnp.sum(fresh_exp, axis=2)
        summed = jnp.einsum(
            "htk,khd->thd",
            cached_exp.astype(jnp.bfloat16),
            value_piece,
            preferred_element_type=jnp.float32,
        )
        summed = summed + jnp.einsum(
            "htk,khd->thd",
            fresh_exp.astype(jnp.bfloat16),
            fresh_value_piece,
            preferred_element_type=jnp.float32,
        )
        return (largest, total_weight, summed.reshape(tok_rows, group_size * HEAD_DIM))

    largest, total_weight, summed = lax.map(head_group, jnp.arange(group_count, dtype=jnp.int32))
    largest, total_weight, summed = merged((largest, total_weight, summed), "col", combine_parts)
    attended = divide_rows(summed, total_weight).astype(jnp.bfloat16)
    projected = jnp.einsum(
        "gtx,gxo->to",
        attended,
        out_weight.reshape(group_count, group_size * HEAD_DIM, feature_width),
        preferred_element_type=jnp.float32,
    )
    attn_out = projected.astype(jnp.bfloat16)
    middle = (residual + residual_scale * attn_out.astype(jnp.float32)).astype(jnp.bfloat16)
    middle_wide = middle.astype(jnp.float32)
    squares_two = lax.psum(jnp.sum(middle_wide * middle_wide, axis=1), "col")
    scale_two = lax.rsqrt(squares_two / D + norm_epsilon)
    moe_normed_f = middle_wide * scale_two[:, None] * moe_gain[None, :]
    logits = lax.psum(jnp.dot(moe_normed_f, router_weight, precision=lax.Precision.HIGHEST), "col")
    moe_normed = moe_normed_f.astype(jnp.bfloat16)
    expert_local = expert_gate.shape[0]
    expert_total = expert_local * row_devices
    capacity = 2 * TOP * tok_rows // expert_total
    onehot_three = (
        routed_experts[:, :, None] == jnp.arange(expert_total, dtype=jnp.int32)[None, None, :]
    )
    selected_logits = jnp.sum(jnp.where(onehot_three, logits[:, None, :], 0.0), axis=2)
    first_gate = jax.nn.sigmoid(selected_logits[:, 0] - selected_logits[:, 1])
    gate_pair = jnp.stack([first_gate, 1.0 - first_gate], axis=1)
    onehot = onehot_three.astype(jnp.int32).reshape(tok_rows * TOP, expert_total)
    earlier = jnp.cumsum(onehot, axis=0, dtype=jnp.int32) - onehot
    slot_index = jnp.sum(earlier * onehot, axis=1, dtype=jnp.int32)
    target = routed_experts.reshape(tok_rows * TOP) * capacity + slot_index
    token_local = jnp.arange(tok_rows * TOP, dtype=jnp.int32) // TOP
    source = jnp.zeros((expert_total * capacity,), jnp.int32).at[target].set(token_local)
    filled = jnp.zeros((expert_total * capacity,), jnp.int32).at[target].set(1)
    outgoing = jnp.where(
        filled[:, None] > 0, moe_normed[source], jnp.zeros((), jnp.bfloat16)
    ).reshape(expert_total, capacity, feature_width)
    arrived = lax.all_to_all(outgoing, "row", split_axis=0, concat_axis=0, tiled=True)
    expert_rows = (
        arrived.reshape(row_devices, expert_local, capacity, feature_width)
        .transpose(1, 0, 2, 3)
        .reshape(expert_local, row_devices * capacity, feature_width)
    )
    feature_piece = lax.all_gather(expert_rows, "col", axis=2, tiled=True)
    gate_next = jnp.einsum(
        "erd,edf->erf", feature_piece, expert_gate, preferred_element_type=jnp.float32
    )
    up_next = jnp.einsum(
        "erd,edf->erf", feature_piece, expert_up, preferred_element_type=jnp.float32
    )
    hidden = (jax.nn.silu(gate_next) * up_next).astype(jnp.bfloat16)
    received_rows = hidden.shape[1]
    value_partial_sum = jnp.einsum(
        "efo,erf->oer", expert_down, hidden, preferred_element_type=jnp.float32
    )
    expert_out = lax.psum_scatter(
        value_partial_sum.reshape(
            lax.axis_size("col") * feature_width, expert_local * received_rows
        ).astype(jnp.bfloat16),
        "col",
        scatter_dimension=0,
        tiled=True,
    )
    returned = lax.all_to_all(
        expert_out.reshape(feature_width, expert_local, received_rows),
        "row",
        split_axis=2,
        concat_axis=1,
        tiled=True,
    )
    flat_back = returned.reshape(feature_width, expert_total * capacity)
    picked = (
        jnp.take(flat_back, target, axis=1)
        .astype(jnp.float32)
        .reshape(feature_width, tok_rows, TOP)
    )
    moe_columns = jnp.sum(picked * gate_pair[None, :, :], axis=2).astype(jnp.bfloat16)
    moe_out = moe_columns.T
    layer_out = (middle_wide + residual_scale * moe_out.astype(jnp.float32)).astype(jnp.bfloat16)
    return (attn_out, moe_out, layer_out)


def solution(mesh):
    in_specs = (
        P("row", "col"),
        P("col"),
        P("col", None),
        P(None, "col"),
        P("col"),
        P("col", None),
        P("row", None, "col"),
        P("row", None, "col"),
        P("row", "col", None),
        P(("row", "col"), None, None),
        P(("row", "col"), None, None),
        P("row", None, None),
        P("row", None),
        P("row", None),
        P("row", None),
    )
    out_specs = (P("row", "col"), P("row", "col"), P("row", "col"))
    return jax.shard_map(
        on_device, mesh=mesh, in_specs=in_specs, out_specs=out_specs, check_vma=False
    )
```

profile of v0, /device:TPU:2, one launch (start us, length us, event | category | flops | bytes accessed | tf_op | source)
XLA Modules:
  0.0 942.3 jit_solution(6926186442801343392)
XLA Ops:
  8.0 62.3 %psum.28 = f32[128]{0:T(128)S(1)} all-reduce(f32[128]{0:T(128)S(1)} %fusion.64), channel_id=1, replica_groups=mesh['row'=8,'col'=32] {'col'}, use_global_device_ids=true, to_apply=%region_1.2 | all-reduce | flops 128 | bytes 1024 | tf_op jit(solution)/shard_map/psum | solution.py:114
  70.3 2.7 convolution_convert_fusion
  77.7 5.0 reshape.454
  82.7 6.9 copy.162
  89.5 5.0 reshape.455
  94.5 6.7 copy.163
  102.5 88.4 %all-reduce.6.cloned.1.call-done = bf16[128,4608]{1,0:T(8,128)(2,1)} async-done(((bf16[128,4608]{1,0:T(8,128)(2,1)}), bf16[128,4608]{1,0:T(8,128)(2,1)}) %all-reduce.6.cloned.1.call-update) | async-done | bytes 1179664
  192.2 117.1 %all-reduce.4.cloned.1.call-done = f32[128,36,64]{0,2,1:T(8,128)} async-done(((f32[128,36,64]{0,2,1:T(8,128)}), f32[128,36,64]{0,2,1:T(8,128)}) %all-reduce.4.cloned.1.call-update) | async-done | bytes 1179664 | tf_op jit(solution)/shard_map/psum | solution.py:118
  310.9 51.9 %while.31 = (s32[]{:T(128)}, f32[9,4,128]{2,1,0:T(4,128)S(1)}, f32[9,4,128]{2,1,0:T(4,128)S(1)}, f32[9,128,256]{2,1,0:T(8,128)}, s32[9]{0:T(128)S(1)}, /*index=5...) while((s32[]{:T(128)}, f32[9,4,128]{2,1,0:T(4,128)S(1)}, ...), condition=%wide.region_16.17_spmd.clone.clone, body=%wide.region_11.16_spmd.clone.clone.sunk | while | flops 69911040 | bytes 5058339 | solution.py:212
  368.0 24.4 %all-gather = f32[288,4,128]{2,1,0:T(4,128)S(1)} all-gather(f32[9,4,128]{2,1,0:T(4,128)S(1)} %get-tuple-element.105), channel_id=2, replica_groups=mesh['row'=8,'col'=32] {'col'}, dimensions={0}, use_global_device_ids=true | all-gather | bytes 608256 | tf_op jit(solution)/shard_map/all_gather | solution.py:17
  392.5 25.6 %all-gather.1 = f32[288,4,128]{2,1,0:T(4,128)S(1)} all-gather(f32[9,4,128]{2,1,0:T(4,128)S(1)} %get-tuple-element.106), channel_id=3, replica_groups=mesh['row'=8,'col'=32] {'col'}, dimensions={0}, use_global_device_ids=true | all-gather | bytes 608256 | tf_op jit(solution)/shard_map/all_gather | solution.py:17
  418.2 76.0 %all-gather.8.cloned.1.call-done = f32[288,128,256]{2,1,0:T(8,128)} async-done(((f32[9,128,256]{2,1,0:T(8,128)}), f32[288,128,256]{2,1,0:T(8,128)}) %all-gather.8.cloned.1.call-update) | async-done | bytes 37748752 | tf_op jit(solution)/shard_map/all_gather | solution.py:17
  496.8 26.9 %slice.93 = f32[279,128,256]{2,1,0:T(8,128)} slice(f32[288,128,256]{2,1,0:T(8,128)} %all-gather.8.cloned.1.call-done), slice={[9:288], [0:128], [0:256]} | slice | bytes 73138176 | tf_op jit(solution)/shard_map/slice | solution.py:19
  523.7 168.2 %while.30 = (s32[]{:T(128)}, f32[9,4,128]{2,1,0:T(4,128)S(1)}, f32[9,4,128]{2,1,0:T(4,128)S(1)}, f32[9,128,256]{1,2,0:T(8,128)}, f32[31,9,4,128]{3,2,1,0:T(4,128...) while((s32[]{:T(128)}, f32[9,4,128]{2,1,0:T(4,128)S(1)}, ...), condition=%wide.region_18.19_spmd, body=%wide.region_17.18_spmd.sunk | while | flops 916994 | bytes 17676496 | solution.py:20
  531.9 2.6 fusion.111
  694.2 60.6 %psum.30 = f32[128]{0:T(128)S(1)} all-reduce(f32[128]{0:T(128)S(1)} %get-tuple-element.401), channel_id=1, replica_groups=mesh['row'=8,'col'=32] {'col'}, use_global_device_ids=true, to_apply=%region_24.25 | all-reduce | flops 128 | bytes 1024 | tf_op jit(solution)/shard_map/psum | solution.py:224
  756.5 15.9 %all_to_all.14 = bf16[8,64,72]{2,1,0:T(8,128)(2,1)S(1)} all-to-all(bf16[8,64,72]{2,1,0:T(8,128)(2,1)S(1)} %broadcast_select_fusion), channel_id=1, replica_groups=mesh['row'=8,'col'=32] {'row'}, dimensions={0} | all-to-all | bytes 147456 | tf_op jit(solution)/shard_map/all_to_all | solution.py:248
  773.2 44.9 %all-gather.6.cloned.1.call-done = bf16[1,512,2304]{1,2,0:T(8,128)(2,1)} async-done(((bf16[1,512,72]{1,2,0:T(8,128)(2,1)}), bf16[1,512,2304]{1,2,0:T(8,128)(2,1)}) %all-gather.6.cloned.1.call-update) | async-done | bytes 2359312 | tf_op jit(solution)/shard_map/all_gather | solution.py:254
  818.1 3.0 fusion.36
  821.2 3.4 fusion.33
  827.9 60.4 %psum.31 = f32[128,8]{0,1:T(8,128)S(1)} all-reduce(f32[128,8]{0,1:T(8,128)S(1)} %fusion.70), channel_id=1, replica_groups=mesh['row'=8,'col'=32] {'col'}, use_global_device_ids=true, to_apply=%region_27.28 | all-reduce | flops 1024 | bytes 8192 | tf_op jit(solution)/shard_map/psum | solution.py:227
  888.4 25.3 %reduce-scatter.4.cloned.1.call-done = bf16[72,512]{1,0:T(8,128)(2,1)} async-done(((bf16[2304,512]{1,0:T(8,128)(2,1)}), bf16[72,512]{1,0:T(8,128)(2,1)}) %reduce-scatter.4.cloned.1.call-update) | async-done | bytes 73744
  917.8 7.0 all-to-all-start.1
  925.0 8.3 all-to-all-done.1
  (695 shorter events, 240.1 us)
Async XLA Ops:
  7.2 814.0 %copy-start = (bf16[1,180,2304]{2,1,0:T(8,128)(2,1)S(1)}, bf16[1,180,2304]{2,1,0:T(8,128)(2,1)}, u32[]{:S(2)}) copy-start(bf16[1,180,2304]{2,1,0:T(8,128)(2,1)} %param.27) | copy-start | bytes 2488324
  7.2 183.7 %all-reduce.6.cloned.1.call-start = ((), (), s32[]{:S(2)}) async-start(), calls=%async_computation.7 | async-start | bytes 2359296
  70.3 2.9 copy-start.8
  70.3 2.9 copy-start.12
  73.1 2.9 copy-start.17
  73.1 3.2 copy-start.14
  73.1 3.4 copy-start.11
  73.1 4.6 copy-start.1
  73.1 236.2 %all-reduce.4.cloned.1.call-start = ((), (), s32[]{:S(2)}) async-start(), calls=%async_computation.3 | async-start | bytes 2359296 | tf_op jit(solution)/shard_map/psum | solution.py:118
  75.8 418.3 %all-gather.8.cloned.1.call-start = ((), (), s32[]{:S(2)}) async-start(), calls=%async_computation.5 | async-start | bytes 38928384 | tf_op jit(solution)/shard_map/all_gather | solution.py:17
  82.7 6.9 copy-start.2
  94.5 6.7 copy-start.18
  362.8 455.3 %all-gather.6.cloned.1.call-start = ((), (), s32[]{:S(2)}) async-start(), calls=%async_computation.4 | async-start | bytes 2433024 | tf_op jit(solution)/shard_map/all_gather | solution.py:254
  526.5 2.6 copy-start.4
  531.9 2.6 copy-start.4
  537.3 2.6 copy-start.4
  542.8 2.6 copy-start.4
  548.2 2.6 copy-start.4
  553.6 2.6 copy-start.4
  651.3 2.6 copy-start.4
  691.9 62.9 %copy-start.13 = (f32[72]{0:T(128)S(1)}, f32[72]{0:T(128)}, u32[]{:S(2)}) copy-start(f32[72]{0:T(128)} %param.23) | copy-start | bytes 868
  694.2 123.9 %copy-start.15 = (bf16[1,2304,180]{1,2,0:T(8,128)(2,1)S(1)}, bf16[1,2304,180]{1,2,0:T(8,128)(2,1)}, u32[]{:S(2)}) copy-start(bf16[1,2304,180]{1,2,0:T(8,128)(2,1)} %param.25) | copy-start | bytes 2488324
  773.1 140.5 %reduce-scatter.4.cloned.1.call-start = ((), (), s32[]{:S(2)}) async-start(), calls=%async_computation.6 | async-start | bytes 2433024
  917.8 15.5 %all-to-all-start.1 = ((bf16[8,2,2304]{2,1,0:T(2,128)(2,1)}), bf16[8,2,2304]{2,1,0:T(2,128)(2,1)S(1)}, u32[]{:S(2)}, u32[]{:S(2)}) async-start(bf16[8,2,2304]{2,1,0:T(2,128)(2,1)} %reshape.465), calls=%async_computation.1 | async-start | bytes 147456 | tf_op jit(solution)/shard_map/all_to_all | solution.py:274
  (122 other events, 206.0 us)
Sparse Core Ops, SparseCore 0:
  73.2 117.6 all-reduce.5
  194.2 115.0 all-reduce.3
  362.9 131.1 all-gather.7
  773.3 44.8 all-gather.5
  827.2 86.4 reduce-scatter.3
where the time goes:
time: 946 us; the launch traced here: 942 us
  waiting for transfers between devices  360 us (38%)
  blocking collectives  249 us (26%)
  local copies, waits for them, and re-layouts  164 us (17%)
  other arithmetic  97.8 us (10%)
  matrix products  40.8 us (4%)
  between operations  14.9 us (2%)
    psum x1, waiting for transfers between devices, on_device(): query_sum = lax.psum(query_part, 'col')  117 us
    unnamed x7, waiting for transfers between devices  114 us
    add x31, other arithmetic, combine_parts(): rescale(earlier_part[2], factor_one) + rescale(later_part[2], factor_two)  81.3 us
    all_gather x1, waiting for transfers between devices, merged(): pieces = jax.tree.map(lambda part: lax.all_gather(part, axis), value)  76 us
    psum x1, blocking collectives, on_device(): squares = lax.psum(jnp.sum(residual * residual, axis=1), 'col')  62.3 us
    psum x1, blocking collectives, on_device(): squares_two = lax.psum(jnp.sum(middle_wide * middle_wide, axis=1), 'col')  60.6 us
    psum x1, blocking collectives, on_device(): lax.psum(jnp.dot(moe_normed_f, router_weight, precision=lax.Precision.HIG...  60.4 us
    dynamic_slice x62, local copies, waits for them, and re-layouts, merged(): lax.scan(lambda running, slab: (join(running, slab), None), head, tail)  53.9 us
  transfers between devices with their start and end apart: 6, of which 6 were waited for; matrix products, arithmetic and copies ran while one was open for 4% of the time, Pallas kernels for 0%

commit v1 on v0

--- a/solution.py
+++ b/solution.py
@@ -251,7 +251,10 @@
         .transpose(1, 0, 2, 3)
         .reshape(expert_local, row_devices * capacity, feature_width)
     )
-    feature_piece = lax.all_gather(expert_rows, "col", axis=2, tiled=True)
+    map_frame = lambda tile_in: jnp.concatenate(
+        lax.all_to_all(jnp.stack([tile_in for _ in range(lax.axis_size("col"))]), "col", 0, 0), 2
+    )
+    feature_piece = map_frame(expert_rows)
     gate_next = jnp.einsum(
         "erd,edf->erf", feature_piece, expert_gate, preferred_element_type=jnp.float32
     )

time: 946 us -> 934 us (0.987)
  waiting for transfers between devices: 360 us -> 309 us
  blocking collectives: 249 us -> 288 us
    all_gather x1 -> x0, waiting for transfers between devices: 44.9 us -> none  [on_device(): feature_piece = lax.all_gather(expert_rows, 'col', axis=2, tiled=True)]
    all_to_all x0 -> x1, blocking collectives: none -> 38.5 us  [on_device(): lax.all_to_all(jnp.stack([tile_in for _ in range(lax.axis_size('col'))]),...]
    unnamed x7 -> x6, waiting for transfers between devices: 114 us -> 108 us
  transfers between devices with their start and end apart: 6 -> 5, of which waited for: 6 -> 5; matrix products, arithmetic and copies ran while one was open for 4% -> 4% of each run, Pallas kernels for 0% -> 0%
where the time goes in v1:
time: 934 us; the launch traced here: 930 us
  waiting for transfers between devices  309 us (33%)
  blocking collectives  288 us (31%)
  local copies, waits for them, and re-layouts  165 us (18%)
  other arithmetic  97.8 us (10%)
  matrix products  39.9 us (4%)
  between operations  14.9 us (2%)
    psum x1, waiting for transfers between devices, on_device(): query_sum = lax.psum(query_part, 'col')  117 us
    unnamed x6, waiting for transfers between devices  108 us
    add x31, other arithmetic, combine_parts(): rescale(earlier_part[2], factor_one) + rescale(later_part[2], factor_two)  81.3 us
    all_gather x1, waiting for transfers between devices, merged(): pieces = jax.tree.map(lambda part: lax.all_gather(part, axis), value)  76 us
    psum x1, blocking collectives, on_device(): squares = lax.psum(jnp.sum(residual * residual, axis=1), 'col')  62.3 us
    psum x1, blocking collectives, on_device(): lax.psum(jnp.dot(moe_normed_f, router_weight, precision=lax.Precision.HIG...  60.5 us
    psum x1, blocking collectives, on_device(): squares_two = lax.psum(jnp.sum(middle_wide * middle_wide, axis=1), 'col')  60.4 us
    dynamic_slice x62, local copies, waits for them, and re-layouts, merged(): lax.scan(lambda running, slab: (join(running, slab), None), head, tail)  53.9 us
  transfers between devices with their start and end apart: 5, of which 5 were waited for; matrix products, arithmetic and copies ran while one was open for 4% of the time, Pallas kernels for 0%

profile of v1, /device:TPU:2, one launch (start us, length us, event | category | flops | bytes accessed | tf_op | source)
XLA Modules:
  0.0 930.1 jit_solution(11281973681035238674)
XLA Ops:
  8.0 62.3 %psum.28 = f32[128]{0:T(128)S(1)} all-reduce(f32[128]{0:T(128)S(1)} %fusion.54), channel_id=1, replica_groups=mesh['row'=8,'col'=32] {'col'}, use_global_device_ids=true, to_apply=%region_1.2 | all-reduce | flops 128 | bytes 1024 | tf_op jit(solution)/shard_map/psum | solution.py:114
  70.3 2.7 convolution_convert_fusion
  77.7 5.0 reshape.465
  82.7 6.9 copy.144
  89.5 5.0 reshape.466
  94.5 6.7 copy.145
  102.5 88.4 %all-reduce.6.cloned.1.call-done = bf16[128,4608]{1,0:T(8,128)(2,1)} async-done(((bf16[128,4608]{1,0:T(8,128)(2,1)}), bf16[128,4608]{1,0:T(8,128)(2,1)}) %all-reduce.6.cloned.1.call-update) | async-done | bytes 1179664
  192.2 117.1 %all-reduce.4.cloned.1.call-done = f32[128,36,64]{0,2,1:T(8,128)} async-done(((f32[128,36,64]{0,2,1:T(8,128)}), f32[128,36,64]{0,2,1:T(8,128)}) %all-reduce.4.cloned.1.call-update) | async-done | bytes 1179664 | tf_op jit(solution)/shard_map/psum | solution.py:118
  310.9 51.9 %while.31 = (s32[]{:T(128)}, f32[9,4,128]{2,1,0:T(4,128)S(1)}, f32[9,4,128]{2,1,0:T(4,128)S(1)}, f32[9,128,256]{2,1,0:T(8,128)}, s32[9]{0:T(128)S(1)}, /*index=5...) while((s32[]{:T(128)}, f32[9,4,128]{2,1,0:T(4,128)S(1)}, ...), condition=%wide.region_16.17_spmd.clone.clone, body=%wide.region_11.16_spmd.clone.clone.sunk | while | flops 69911040 | bytes 5058339 | solution.py:212
  368.0 24.4 %all-gather = f32[288,4,128]{2,1,0:T(4,128)S(1)} all-gather(f32[9,4,128]{2,1,0:T(4,128)S(1)} %get-tuple-element.105), channel_id=2, replica_groups=mesh['row'=8,'col'=32] {'col'}, dimensions={0}, use_global_device_ids=true | all-gather | bytes 608256 | tf_op jit(solution)/shard_map/all_gather | solution.py:17
  392.5 25.6 %all-gather.1 = f32[288,4,128]{2,1,0:T(4,128)S(1)} all-gather(f32[9,4,128]{2,1,0:T(4,128)S(1)} %get-tuple-element.106), channel_id=3, replica_groups=mesh['row'=8,'col'=32] {'col'}, dimensions={0}, use_global_device_ids=true | all-gather | bytes 608256 | tf_op jit(solution)/shard_map/all_gather | solution.py:17
  418.2 76.0 %all-gather.5.cloned.1.call-done = f32[288,128,256]{2,1,0:T(8,128)} async-done(((f32[9,128,256]{2,1,0:T(8,128)}), f32[288,128,256]{2,1,0:T(8,128)}) %all-gather.5.cloned.1.call-update) | async-done | bytes 37748752 | tf_op jit(solution)/shard_map/all_gather | solution.py:17
  496.8 26.9 %slice.93 = f32[279,128,256]{2,1,0:T(8,128)} slice(f32[288,128,256]{2,1,0:T(8,128)} %all-gather.5.cloned.1.call-done), slice={[9:288], [0:128], [0:256]} | slice | bytes 73138176 | tf_op jit(solution)/shard_map/slice | solution.py:19
  523.7 168.2 %while.30 = (s32[]{:T(128)}, f32[9,4,128]{2,1,0:T(4,128)S(1)}, f32[9,4,128]{2,1,0:T(4,128)S(1)}, f32[9,128,256]{1,2,0:T(8,128)}, f32[31,9,4,128]{3,2,1,0:T(4,128...) while((s32[]{:T(128)}, f32[9,4,128]{2,1,0:T(4,128)S(1)}, ...), condition=%wide.region_18.19_spmd, body=%wide.region_17.18_spmd.sunk | while | flops 916994 | bytes 17676496 | solution.py:20
  531.9 2.6 fusion.103
  694.2 60.4 %psum.30 = f32[128]{0:T(128)S(1)} all-reduce(f32[128]{0:T(128)S(1)} %get-tuple-element.378), channel_id=1, replica_groups=mesh['row'=8,'col'=32] {'col'}, use_global_device_ids=true, to_apply=%region_24.25 | all-reduce | flops 128 | bytes 1024 | tf_op jit(solution)/shard_map/psum | solution.py:224
  756.4 15.9 %all_to_all.19 = bf16[8,64,72]{2,1,0:T(8,128)(2,1)S(1)} all-to-all(bf16[8,64,72]{2,1,0:T(8,128)(2,1)S(1)} %broadcast_select_fusion), channel_id=1, replica_groups=mesh['row'=8,'col'=32] {'row'}, dimensions={0} | all-to-all | bytes 147456 | tf_op jit(solution)/shard_map/all_to_all | solution.py:248
  772.5 38.5 %all_to_all.20 = bf16[32,1,512,72]{2,3,1,0:T(8,128)(2,1)S(1)} all-to-all(bf16[32,1,512,72]{2,3,1,0:T(8,128)(2,1)S(1)} %stack.8), channel_id=1, replica_groups=mesh['row'=8,'col'=32] {'col'}, dimensions={0} | all-to-all | bytes 4718592 | tf_op jit(solution)/shard_map/all_to_all | solution.py:255
  812.4 4.1 fusion.33
  816.5 4.3 copy.147
  821.7 60.5 %psum.31 = f32[128,8]{0,1:T(8,128)S(1)} all-reduce(f32[128,8]{0,1:T(8,128)S(1)} %fusion.60), channel_id=1, replica_groups=mesh['row'=8,'col'=32] {'col'}, use_global_device_ids=true, to_apply=%region_27.28 | all-reduce | flops 1024 | bytes 8192 | tf_op jit(solution)/shard_map/psum | solution.py:227
  882.2 19.3 %reduce-scatter.4.cloned.1.call-done = bf16[72,512]{1,0:T(8,128)(2,1)} async-done(((bf16[2304,512]{1,0:T(8,128)(2,1)}), bf16[72,512]{1,0:T(8,128)(2,1)}) %reduce-scatter.4.cloned.1.call-update) | async-done | bytes 73744
  905.6 7.0 all-to-all-start.2
  912.7 8.3 all-to-all-done.2
  (694 shorter events, 238.5 us)
Async XLA Ops:
  7.2 805.3 %copy-start = (bf16[1,180,2304]{2,1,0:T(8,128)(2,1)S(1)}, bf16[1,180,2304]{2,1,0:T(8,128)(2,1)}, u32[]{:S(2)}) copy-start(bf16[1,180,2304]{2,1,0:T(8,128)(2,1)} %param.27) | copy-start | bytes 2488324
  7.2 183.7 %all-reduce.6.cloned.1.call-start = ((), (), s32[]{:S(2)}) async-start(), calls=%async_computation.7 | async-start | bytes 2359296
  70.3 2.9 copy-start.8
  70.3 2.9 copy-start.12
  73.1 2.9 copy-start.17
  73.1 3.2 copy-start.14
  73.1 3.4 copy-start.11
  73.1 4.6 copy-start.1
  73.1 236.2 %all-reduce.4.cloned.1.call-start = ((), (), s32[]{:S(2)}) async-start(), calls=%async_computation.4 | async-start | bytes 2359296 | tf_op jit(solution)/shard_map/psum | solution.py:118
  75.8 418.3 %all-gather.5.cloned.1.call-start = ((), (), s32[]{:S(2)}) async-start(), calls=%async_computation.5 | async-start | bytes 38928384 | tf_op jit(solution)/shard_map/all_gather | solution.py:17
  82.7 6.9 copy-start.2
  94.5 6.7 copy-start.18
  362.8 538.7 %reduce-scatter.4.cloned.1.call-start = ((), (), s32[]{:S(2)}) async-start(), calls=%async_computation.6 | async-start | bytes 2433024
  526.5 2.6 copy-start.4
  531.9 2.6 copy-start.4
  537.3 2.6 copy-start.4
  542.8 2.6 copy-start.4
  548.2 2.6 copy-start.4
  553.6 2.6 copy-start.4
  559.0 2.6 copy-start.4
  651.3 2.6 copy-start.4
  691.9 62.8 %copy-start.13 = (f32[72]{0:T(128)S(1)}, f32[72]{0:T(128)}, u32[]{:S(2)}) copy-start(f32[72]{0:T(128)} %param.23) | copy-start | bytes 868
  772.5 38.5 %copy-start.15 = (bf16[1,2304,180]{1,2,0:T(8,128)(2,1)S(1)}, bf16[1,2304,180]{1,2,0:T(8,128)(2,1)}, u32[]{:S(2)}) copy-start(bf16[1,2304,180]{1,2,0:T(8,128)(2,1)} %param.25) | copy-start | bytes 2488324
  905.6 15.4 %all-to-all-start.2 = ((bf16[8,2,2304]{2,1,0:T(2,128)(2,1)}), bf16[8,2,2304]{2,1,0:T(2,128)(2,1)S(1)}, u32[]{:S(2)}, u32[]{:S(2)}) async-start(bf16[8,2,2304]{2,1,0:T(2,128)(2,1)} %reshape.476), calls=%async_computation.2 | async-start | bytes 147456 | tf_op jit(solution)/shard_map/all_to_all | solution.py:277
  (121 other events, 203.3 us)
Sparse Core Ops, SparseCore 0:
  73.2 117.6 all-reduce.5
  194.2 115.0 all-reduce.3
  362.9 131.1 all-gather.4
  821.0 80.5 reduce-scatter.3
